TPU v7x, 32 devices: a whole 2x2x4 slice. The times are simulated.
32 devices in a mesh: tm: 8 (over z, x), row: 4 (over y, core).
Axes of the slice: x: 2, y: 2, z: 4, core: 2. Of those that a mesh axis runs over, the one named last changes fastest.
Arguments:
- coupling: bfloat16 [8, 4096, 2048], P('tm', 'row'), as said below
- row_scale: float32 [8, 4096], P('tm', 'row'), may hold values from 0.1 to 10
- block_mask: int32 [8, 32, 16], P('tm', 'row'), may hold values 0 or 1
- link_map: int32 [8, 16], P('tm'), may hold values from 0 to 15, each once within a row
- tile_order: int32 [16], replicated, may hold values from 0 to 15, each once
- link_diag: float32 [8, 2048], P('tm'), may hold values from 0.1 to 1
Outputs:
- schur_rows: float32 [8, 2048, 2048], P('tm', 'row')
- chain_complement: float32 [8, 3, 128, 128], P('tm')
Inputs may be any that keep to these rules, and one draw needn't show every extreme that they name: `coupling`: entries lie within 6 / sqrt(4096) of zero. Each row of link_map lists every linking block once. tile_order lists every linking block once.
All inputs are finite; a program needn't handle non-finite values. No bound on the sum of `block_mask` on one device may be relied on, other than what follows from the above.
Results may differ from a plain program's by a relative error of at most 0.0011.
Values may be sent and summed in bfloat16 or wider, within the bound.
No kernel may reach another device: no remote copies, remote signals or barrier semaphores. Data moves between devices by JAX's collectives and lax.ppermute only.
A program may use at most 128 MiB of HBM per device.

v0:
```python
import jax
import jax.numpy as jnp
from jax import lax
from jax.sharding import PartitionSpec as P

L = 2048
BLK = 128
HIGHEST = lax.Precision.HIGHEST


def join_segments(earlier_seg, later_seg):
    top_one, cross_one, bottom_one, empty_one = earlier_seg
    top_two, cross_two, bottom_two, empty_two = later_seg
    both_empty = empty_one * empty_two
    middle = bottom_one + top_two
    middle = 0.5 * (middle + middle.T) + both_empty * jnp.eye(middle.shape[0], dtype=jnp.float32)
    factor = jnp.linalg.cholesky(middle)
    half_width = top_one.shape[0]
    solved = jax.scipy.linalg.cho_solve(
        (factor, True), jnp.concatenate([cross_one.T, cross_two], axis=1)
    )
    solve_one = solved[:, :half_width]
    solve_two = solved[:, half_width:]
    top_new = top_one - jnp.dot(cross_one, solve_one, precision=HIGHEST)
    cross_new = -jnp.dot(cross_one, solve_two, precision=HIGHEST)
    bottom_new = bottom_two - jnp.dot(cross_two.T, solve_two, precision=HIGHEST)
    first_empty = empty_one > 0.5
    second_empty = empty_two > 0.5
    top_out = jnp.where(first_empty, top_two, jnp.where(second_empty, top_one, top_new))
    cross_out = jnp.where(first_empty, cross_two, jnp.where(second_empty, cross_one, cross_new))
    bottom_out = jnp.where(first_empty, bottom_two, jnp.where(second_empty, bottom_one, bottom_new))
    return (top_out, cross_out, bottom_out, both_empty)


def contract_rows(left_cols, right_cols):
    return lax.dot_general(
        left_cols, right_cols, (((0,), (0,)), ((), ())), preferred_element_type=jnp.float32
    )


def local(coupling, row_scale, block_mask, link_map, tile_order, link_diag):
    local_slab = coupling[0]
    row_weights = row_scale[0]
    live_blocks = block_mask[0]
    block_map = link_map[0]
    diagonal = link_diag[0]
    slab_height = local_slab.shape[0]
    block_count = L // BLK
    owners = lax.axis_size("row")
    own_blocks = block_count // owners
    own_rows = own_blocks * BLK
    my_index = lax.axis_index("row")
    masked = (
        local_slab.reshape(slab_height // BLK, BLK, block_count, BLK)
        * live_blocks.astype(jnp.bfloat16)[:, None, :, None]
    ).reshape(slab_height, block_count, BLK)
    block_ids = jnp.arange(block_count, dtype=jnp.int32)
    source = jnp.sum(
        block_ids[None, :] * (block_map[None, :] == block_ids[:, None]).astype(jnp.int32), axis=1
    )
    global_cols = jnp.take(masked, source, axis=1).reshape(slab_height, L)
    my_blocks = lax.dynamic_slice_in_dim(tile_order, my_index * own_blocks, own_blocks)
    left_cols = jnp.take(masked, jnp.take(source, tile_order), axis=1).reshape(slab_height, L)
    scaled = (row_weights[:, None] * global_cols.astype(jnp.float32)).astype(jnp.bfloat16)
    owned = lax.psum_scatter(
        contract_rows(left_cols, scaled), "row", scatter_dimension=0, tiled=True
    )
    local_rows = jnp.arange(own_rows, dtype=jnp.int32)
    target = jnp.repeat(my_blocks, BLK) * BLK + local_rows % BLK
    column_ids = jnp.arange(L, dtype=jnp.int32)
    owned = owned + jnp.where(
        column_ids[None, :] == target[:, None], jnp.take(diagonal, target)[:, None], 0.0
    )

    def pick_rows(wanted):
        where_held = jnp.sum(block_ids * (tile_order == wanted).astype(jnp.int32))
        local_block = where_held - my_index * own_blocks
        is_held = (local_block >= 0) & (local_block < own_blocks)
        rows_here = lax.dynamic_slice_in_dim(
            owned, jnp.clip(local_block, 0, own_blocks - 1) * BLK, BLK
        )
        return jnp.where(is_held, rows_here, 0.0)

    first_rows = pick_rows(0)
    final_rows = pick_rows(block_count - 1)
    pieces = (first_rows[:, :BLK], first_rows[:, L - BLK :], final_rows[:, L - BLK :])
    summed = lax.psum((pieces[0], pieces[1], pieces[2]), "row")
    own_segment = (summed[0], summed[1], summed[2], jnp.zeros((), jnp.float32))
    stacked = jnp.stack(own_segment[:3])[None]
    every_segment = lax.all_gather(stacked, "tm", axis=0, tiled=True)
    segment_count = every_segment.shape[0]
    empty_flags = jnp.zeros((segment_count,), jnp.float32)
    prefixes = lax.associative_scan(
        jax.vmap(join_segments),
        (every_segment[:, 0], every_segment[:, 1], every_segment[:, 2], empty_flags),
    )
    position = lax.axis_index("tm")
    chain_out = jnp.stack(
        [lax.dynamic_index_in_dim(member, position, 0, False) for member in prefixes[:3]]
    )[None]
    return (owned[None], chain_out)


def solution(mesh):
    placed = (
        P("tm", "row", None),
        P("tm", "row"),
        P("tm", "row", None),
        P("tm", None),
        P(),
        P("tm", None),
    )
    return jax.shard_map(
        local,
        mesh=mesh,
        in_specs=placed,
        out_specs=(P("tm", "row", None), P("tm", None, None, None)),
        check_vma=False,
    )
```

profile of v0, /device:TPU:0, one launch (start us, length us, event | category | flops | bytes accessed | tf_op | source)
XLA Modules:
  0.0 581.4 jit_solution(10147022563122233437)
XLA Ops:
  7.2 6.4 %copy.204 = bf16[1,1024,2048]{1,2,0:T(8,128)(2,1)} copy(bf16[1,1024,2048]{2,1,0:T(8,128)(2,1)} %param.11) | data formatting | bytes 8388608 | tf_op args[0]
  13.6 6.4 %copy.206 = bf16[1024,16,128]{2,0,1:T(8,128)(2,1)} copy(bf16[1024,16,128]{0,2,1:T(8,128)(2,1)} %bitcast.199) | data formatting | bytes 8388608 | tf_op jit(solution)/shard_map/reshape;squeeze | solution.py:54
  20.4 0.6 fusion.73
  21.1 0.7 gather_fusion
  21.7 5.8 %broadcast_multiply_fusion = bf16[1024,16,128]{2,0,1:T(8,128)(2,1)} fusion(bf16[1024,16,128]{2,0,1:T(8,128)(2,1)} %copy.206, bf16[1024,16]{0,1:T(8,128)(2,1)S(1)} %bitcast.215), kind=kLoop, calls=%fused_computation.8 | loop fusion | flops 2097152 | bytes 8421376 | tf_op jit(solution)/shard_map/mul | solution.py:54
  27.6 5.2 gather_fusion.2
  32.8 4.6 select_bitcast_fusion
  37.3 6.4 %copy.207 = bf16[1024,16,128]{0,2,1:T(8,128)(2,1)} copy(bf16[1024,16,128]{2,0,1:T(8,128)(2,1)} %select_bitcast_fusion) | data formatting | bytes 8388608 | tf_op jit(solution)/shard_map/jit(_take)/select_n | solution.py:63
  43.7 5.2 gather_fusion.3
  49.0 5.7 multiply_convert_fusion
  54.6 6.4 %copy.208 = bf16[1024,16,128]{0,2,1:T(8,128)(2,1)} copy(bf16[1024,16,128]{2,0,1:T(8,128)(2,1)} %multiply_convert_fusion) | data formatting | bytes 8388608 | tf_op jit(solution)/shard_map/convert_element_type | solution.py:64
  61.0 15.2 %fusion.103 = f32[2048,2048]{1,0:T(8,128)} fusion(bf16[1024,2048]{0,1:T(8,128)(2,1)} %bitcast.200, bf16[1024,2048]{0,1:T(8,128)(2,1)} %bitcast.201), kind=kOutput, calls=%fused_computation.217 | convolution fusion | flops 8589934592 | bytes 25165824 | tf_op jit(solution)/shard_map/dot_general | solution.py:36
  77.7 3.1 gather_fusion.1
  81.0 124.1 %reduce-scatter.2.cloned.1.call-done = f32[512,2048]{1,0:T(8,128)} async-done(((f32[2048,2048]{1,0:T(8,128)}), f32[512,2048]{1,0:T(8,128)}) %reduce-scatter.2.cloned.1.call-update) | async-done | bytes 4194320 | tf_op jit(solution)/shard_map/reduce_scatter | solution.py:65
  205.2 2.8 select_add_fusion
  208.0 0.7 slice_bitcast_fusion.8
  208.7 0.6 fusion.53
  209.7 31.8 %all-reduce.21.cloned.1.call-done = (f32[1,128,128]{2,1,0:T(8,128)}, f32[1,128,128]{2,1,0:T(8,128)}, f32[1,128,128]{2,1,0:T(8,128)}) async-done(((f32[1,128,128]{2,1,0:T(8,128)}, f32[1,128,128]{2,1,0:T(8,128)}, f32[1,128,128]{2,1,0:T(8,128)}), (f32[1,128,128]{2,1,0:T(8,128)}, f32[1,128,128]{2,1,0:T(8,128)}, f32[1,128,128]{2,1,0:T(8,128)})) %all-reduce.21.cloned.1.call-update) | async-done | bytes 196624 | tf_op jit(solution)/shard_map/psum | solution.py:87
  241.5 1.6 pad_maximum_fusion.3
  243.1 4.8 fusion.113
  247.9 40.5 %all-gather.3.cloned.1.call-done = f32[24,128,128]{2,1,0:T(8,128)} async-done(((f32[3,128,128]{2,1,0:T(8,128)}), f32[24,128,128]{2,1,0:T(8,128)}) %all-gather.3.cloned.1.call-update) | async-done | bytes 1572880 | tf_op jit(solution)/shard_map/all_gather | solution.py:90
  288.4 1.5 fusion.95
  291.0 46.9 %custom-call.41 = f32[4,128,128]{2,1,0:T(8,128)S(1)} custom-call(f32[4,128,128]{2,1,0:T(8,128)S(1)} %copy.216), custom_call_target="Cholesky" | custom-call | tf_op jit(solution)/shard_map/vmap(jit(cholesky))/cholesky | solution.py:17
  338.2 39.3 %custom-call.42 = f32[4,1,128,128]{2,3,1,0:T(8,128)S(1)} custom-call(f32[4,1,128,128]{3,2,1,0:T(8,128)S(1)} %select_bitcast_fusion.1), custom_call_target="InvertDiagBlocksLowerTriangular" | custom-call | tf_op jit(solution)/shard_map/vmap(jit(_cho_solve))/triangular_solve | solution.py:19
  377.5 0.6 fusion.6
  378.2 0.6 fusion.19
  379.2 0.7 fusion.98
  379.9 0.6 convolution_subtract_fusion.1
  380.6 0.6 convolution_subtract_fusion
  381.7 23.5 %custom-call.43 = f32[2,128,128]{2,1,0:T(8,128)S(1)} custom-call(f32[2,128,128]{2,1,0:T(8,128)S(1)} %fusion.44), custom_call_target="Cholesky" | custom-call | tf_op jit(solution)/shard_map/vmap(jit(cholesky))/cholesky | solution.py:17
  405.4 28.4 %custom-call.44 = f32[2,1,128,128]{2,3,1,0:T(8,128)S(1)} custom-call(f32[2,1,128,128]{3,2,1,0:T(8,128)S(1)} %select_bitcast_fusion.3), custom_call_target="InvertDiagBlocksLowerTriangular" | custom-call | tf_op jit(solution)/shard_map/vmap(jit(_cho_solve))/triangular_solve | solution.py:19
  435.9 0.6 fusion.101
  436.7 11.7 %custom-call.49 = f32[1,128,128]{2,1,0:T(8,128)S(1)} custom-call(f32[1,128,128]{2,1,0:T(8,128)S(1)} %fusion.66), custom_call_target="Cholesky" | custom-call | tf_op jit(solution)/shard_map/vmap(jit(cholesky))/cholesky | solution.py:17
  448.5 0.6 compare_reduce_fusion.1
  449.1 0.7 fusion.48
  449.8 9.8 %custom-call.50 = f32[1,1,128,128]{2,3,1,0:T(8,128)S(1)} custom-call(f32[1,1,128,128]{3,2,1,0:T(8,128)S(1)} %fusion.48), custom_call_target="InvertDiagBlocksLowerTriangular" | custom-call | tf_op jit(solution)/shard_map/vmap(jit(_cho_solve))/triangular_solve | solution.py:19
  460.8 0.6 slice.343
  461.4 0.7 slice.295
  462.2 0.6 fusion.97
  463.1 11.9 %custom-call.51 = f32[1,128,128]{2,1,0:T(8,128)S(1)} custom-call(f32[1,128,128]{2,1,0:T(8,128)S(1)} %fusion.59), custom_call_target="Cholesky" | custom-call | tf_op jit(solution)/shard_map/vmap(jit(cholesky))/cholesky | solution.py:17
  475.0 0.6 compare_reduce_fusion
  475.6 0.6 fusion.49
  476.2 9.8 %custom-call.52 = f32[1,1,128,128]{2,3,1,0:T(8,128)S(1)} custom-call(f32[1,1,128,128]{3,2,1,0:T(8,128)S(1)} %fusion.49), custom_call_target="InvertDiagBlocksLowerTriangular" | custom-call | tf_op jit(solution)/shard_map/vmap(jit(_cho_solve))/triangular_solve | solution.py:19
  486.0 1.1 fusion.38
  488.0 0.9 pad_maximum_fusion.6
  489.0 0.7 slice_add_fusion.1
  489.7 1.6 fusion.94
  491.3 0.9 pad_maximum_fusion.5
  492.3 0.7 add_bitcast_fusion
  493.0 1.1 copy.243
  494.5 35.2 %custom-call.45 = f32[3,128,128]{2,1,0:T(8,128)S(1)} custom-call(f32[3,128,128]{2,1,0:T(8,128)S(1)} %fusion.30), custom_call_target="Cholesky" | custom-call | tf_op jit(solution)/shard_map/vmap(jit(cholesky))/cholesky | solution.py:17
  529.7 0.8 select_reduce_fusion.1
  530.6 0.8 select_bitcast_fusion.2
  531.4 29.5 %custom-call.46 = f32[3,1,128,128]{2,3,1,0:T(8,128)S(1)} custom-call(f32[3,1,128,128]{3,2,1,0:T(8,128)S(1)} %select_bitcast_fusion.2), custom_call_target="InvertDiagBlocksLowerTriangular" | custom-call | tf_op jit(solution)/shard_map/vmap(jit(_cho_solve))/triangular_solve | solution.py:19
  560.9 1.5 fusion.10
  562.9 0.5 convolution_subtract_fusion.3
  563.5 0.5 convolution_negate_fusion.1
  565.6 0.9 copy.286
  566.6 0.9 copy.285
  567.6 2.1 pad.77
  569.7 2.1 pad.76
  572.0 0.9 dynamic-slice_add_fusion.1
  572.9 0.8 dynamic-slice_add_fusion.2
  573.7 0.8 copy.256
  (137 shorter events, 11.3 us)
Async XLA Ops:
  7.2 70.6 %copy-start = (f32[1,2048]{1,0:T(1,128)S(1)}, f32[1,2048]{1,0:T(1,128)}, u32[]{:S(2)}) copy-start(f32[1,2048]{1,0:T(1,128)} %param.16) | copy-start | bytes 24580
  7.2 198.0 %reduce-scatter.2.cloned.1.call-start = ((), (), s32[]{:S(2)}) async-start(), calls=%async_computation.1 | async-start | bytes 20971520 | tf_op jit(solution)/shard_map/reduce_scatter | solution.py:65
  13.6 6.4 %copy-start.7 = (s32[1,8,16]{2,1,0:T(8,128)S(1)}, s32[1,8,16]{2,1,0:T(8,128)}, u32[]{:S(2)}) copy-start(s32[1,8,16]{2,1,0:T(8,128)} %param.13) | copy-start | bytes 1540
  13.6 6.6 %copy-start.9 = (s32[1,16]{1,0:T(1,128)S(1)}, s32[1,16]{1,0:T(1,128)}, u32[]{:S(2)}) copy-start(s32[1,16]{1,0:T(1,128)} %param.14) | copy-start | bytes 196
  13.6 6.8 %copy-start.8 = (s32[16]{0:T(128)S(1)}, s32[16]{0:T(128)}, u32[]{:S(2)}) copy-start(s32[16]{0:T(128)} %param.15) | copy-start | bytes 196
  43.7 5.2 copy-start.6
  76.2 165.3 %all-reduce.21.cloned.1.call-start = ((), (), s32[]{:S(2)}) async-start(), calls=%async_computation.3 | async-start | bytes 393216 | tf_op jit(solution)/shard_map/psum | solution.py:87
  209.4 79.1 %all-gather.3.cloned.1.call-start = ((), (), s32[]{:S(2)}) async-start(), calls=%async_computation.2 | async-start | bytes 1769472 | tf_op jit(solution)/shard_map/all_gather | solution.py:90
  243.1 162.1 %copy-start.3 = (pred[128,128]{1,0:T(8,128)(4,1)}, pred[128,128]{1,0:T(8,128)(4,1)S(1)}, u32[]{:S(2)}) copy-start(pred[128,128]{1,0:T(8,128)(4,1)S(1)} %iota_compare_fusion.3) | copy-start | bytes 49156
  243.1 162.2 %copy-start.1 = (pred[128,128]{1,0:T(8,128)(4,1)}, pred[128,128]{1,0:T(8,128)(4,1)S(1)}, u32[]{:S(2)}) copy-start(pred[128,128]{1,0:T(8,128)(4,1)S(1)} %iota_compare_fusion.4) | copy-start | bytes 49156
  493.0 71.2 %copy-start.4 = (f32[1,128,128]{2,1,0:T(8,128)S(1)}, f32[1,128,128]{2,1,0:T(8,128)}, u32[]{:S(2)}) copy-start(f32[1,128,128]{2,1,0:T(8,128)} %get-tuple-element.42) | copy-start | bytes 196612
  494.1 70.6 %copy-start.2 = (f32[1,128,128]{1,2,0:T(8,128)S(1)}, f32[1,128,128]{1,2,0:T(8,128)}, u32[]{:S(2)}) copy-start(f32[1,128,128]{1,2,0:T(8,128)} %get-tuple-element.34) | copy-start | bytes 196612
  564.4 7.4 %copy-start.5 = (f32[1,1,128,128]{3,2,1,0:T(8,128)S(1)}, f32[1,1,128,128]{3,2,1,0:T(8,128)}, u32[]{:S(2)}) copy-start(f32[1,1,128,128]{3,2,1,0:T(8,128)} %get-tuple-element.22) | copy-start | bytes 196612
Sparse Core Ops, SparseCore 0:
  76.3 128.8 reduce-scatter.1
  209.5 31.9 all-reduce.20
  244.2 44.1 all-gather.2
where the time goes:
time: 590 us; the launch traced here: 581 us
  other arithmetic  284 us (48%)
  waiting for transfers between devices  197 us (33%)
  local copies, waits for them, and re-layouts  57.1 us (10%)
  matrix products  26.8 us (5%)
  between operations  16.4 us (3%)
    another operation x16, other arithmetic, join_segments(): factor = jnp.linalg.cholesky(middle)  132 us
    reduce_scatter x1, waiting for transfers between devices, local(): lax.psum_scatter(contract_rows(left_cols, scaled), 'row', scatter_dimensi...  124 us
    another operation x11, other arithmetic, join_segments(): jax.scipy.linalg.cho_solve((factor, True), jnp.concatenate([cross_one.T,...  119 us
    all_gather x1, waiting for transfers between devices, local(): every_segment = lax.all_gather(stacked, 'tm', axis=0, tiled=True)  40.5 us
    psum x1, waiting for transfers between devices, local(): summed = lax.psum((pieces[0], pieces[1], pieces[2]), 'row')  31.8 us
    dot_general x1, matrix products, contract_rows(): lax.dot_general(left_cols, right_cols, (((0,), (0,)), ((), ())), preferre...  15.2 us
  transfers between devices with their start and end apart: 3, of which 3 were waited for; matrix products, arithmetic and copies ran while one was open for 1% of the time, Pallas kernels for 0%

commit v1 on v0

--- a/solution.py
+++ b/solution.py
@@ -87,7 +87,24 @@
     summed = lax.psum((pieces[0], pieces[1], pieces[2]), "row")
     own_segment = (summed[0], summed[1], summed[2], jnp.zeros((), jnp.float32))
     stacked = jnp.stack(own_segment[:3])[None]
-    every_segment = lax.all_gather(stacked, "tm", axis=0, tiled=True)
+    size, index, width = (lax.axis_size("tm"), lax.axis_index("tm"), stacked.shape[0])
+    upward = [(i, (i + 1) % size) for i in range(size)]
+    behind = [(i, (i - 1) % size) for i in range(size)]
+    whole = jnp.zeros((*stacked.shape[:0], size * width, *stacked.shape[0 + 1 :]), stacked.dtype)
+    whole = lax.dynamic_update_slice_in_dim(whole, stacked, index * width, axis=0)
+    from_left = from_right = stacked
+    halfway = size // 2
+    for step in range(1, halfway + 1):
+        from_left = lax.ppermute(from_left, "tm", upward)
+        whole = lax.dynamic_update_slice_in_dim(
+            whole, from_left, (index - step) % size * width, axis=0
+        )
+        if step < size - halfway:
+            from_right = lax.ppermute(from_right, "tm", behind)
+            whole = lax.dynamic_update_slice_in_dim(
+                whole, from_right, (index + step) % size * width, axis=0
+            )
+    every_segment = whole
     segment_count = every_segment.shape[0]
     empty_flags = jnp.zeros((segment_count,), jnp.float32)
     prefixes = lax.associative_scan(

time: 590 us -> 623 us (1.056)
  waiting for transfers between devices: 197 us -> 172 us
  starting transfers between devices: 0.38 us -> 18.9 us
  local copies, waits for them, and re-layouts: 57.1 us -> 73.7 us
  matrix products: 26.8 us -> 38.1 us
  other arithmetic: 284 us -> 292 us
    all_gather x1 -> x0, waiting for transfers between devices: 40.5 us -> none  [local(): every_segment = lax.all_gather(stacked, 'tm', axis=0, tiled=True)]
    ppermute x0 -> x7, starting transfers between devices: none -> 18.8 us  [the longest x3 9.63 us: local(): from_right = lax.ppermute(from_right, 'tm', behind)]
    ppermute x0 -> x7, waiting for transfers between devices: none -> 15.5 us  [the longest x4 14 us: local(): from_left = lax.ppermute(from_left, 'tm', upward)]
    unnamed x40 -> x62, local copies, waits for them, and re-layouts: 10.7 us -> 17.2 us
    another operation x11, other arithmetic: 119 us -> 113 us  [join_segments(): jax.scipy.linalg.cho_solve((factor, True), jnp.concatenate([cross_one.T,...]
  transfers between devices with their start and end apart: 3 -> 9, of which waited for: 3 -> 7; matrix products, arithmetic and copies ran while one was open for 1% -> 1% of each run, Pallas kernels for 0% -> 0%
where the time goes in v1:
time: 623 us; the launch traced here: 611 us
  other arithmetic  292 us (47%)
  waiting for transfers between devices  172 us (28%)
  local copies, waits for them, and re-layouts  73.7 us (12%)
  matrix products  38.1 us (6%)
  starting transfers between devices  18.9 us (3%)
  between operations  16.9 us (3%)
    another operation x16, other arithmetic, join_segments(): factor = jnp.linalg.cholesky(middle)  135 us
    reduce_scatter x1, waiting for transfers between devices, local(): lax.psum_scatter(contract_rows(left_cols, scaled), 'row', scatter_dimensi...  124 us
    another operation x11, other arithmetic, join_segments(): jax.scipy.linalg.cho_solve((factor, True), jnp.concatenate([cross_one.T,...  113 us
    psum x1, waiting for transfers between devices, local(): summed = lax.psum((pieces[0], pieces[1], pieces[2]), 'row')  32.1 us
    unnamed x62, local copies, waits for them, and re-layouts  17.2 us
    dot_general x1, matrix products, contract_rows(): lax.dot_general(left_cols, right_cols, (((0,), (0,)), ((), ())), preferre...  15.3 us
    ppermute x4, waiting for transfers between devices, local(): from_left = lax.ppermute(from_left, 'tm', upward)  14 us
  transfers between devices with their start and end apart: 9, of which 7 were waited for; matrix products, arithmetic and copies ran while one was open for 1% of the time, Pallas kernels for 0%

profile of v1, /device:TPU:0, one launch (start us, length us, event | category | flops | bytes accessed | tf_op | source)
XLA Modules:
  0.0 611.3 jit_solution(3872235796368012731)
XLA Ops:
  7.2 6.4 %copy.149 = bf16[1,1024,2048]{1,2,0:T(8,128)(2,1)} copy(bf16[1,1024,2048]{2,1,0:T(8,128)(2,1)} %param.11) | data formatting | bytes 8388608 | tf_op args[0]
  13.6 6.4 %copy.151 = bf16[1024,16,128]{2,0,1:T(8,128)(2,1)} copy(bf16[1024,16,128]{0,2,1:T(8,128)(2,1)} %bitcast.204) | data formatting | bytes 8388608 | tf_op jit(solution)/shard_map/reshape;squeeze | solution.py:54
  21.8 5.8 broadcast_multiply_fusion
  27.6 5.2 gather_fusion.2
  32.8 4.6 select_bitcast_fusion
  37.4 6.4 %copy.152 = bf16[1024,16,128]{0,2,1:T(8,128)(2,1)} copy(bf16[1024,16,128]{2,0,1:T(8,128)(2,1)} %select_bitcast_fusion) | data formatting | bytes 8388608 | tf_op jit(solution)/shard_map/jit(_take)/select_n | solution.py:63
  43.8 5.2 gather_fusion.3
  49.1 5.7 multiply_convert_fusion
  54.7 6.4 %copy.153 = bf16[1024,16,128]{0,2,1:T(8,128)(2,1)} copy(bf16[1024,16,128]{2,0,1:T(8,128)(2,1)} %multiply_convert_fusion) | data formatting | bytes 8388608 | tf_op jit(solution)/shard_map/convert_element_type | solution.py:64
  61.1 15.3 %fusion.113 = f32[2048,2048]{1,0:T(8,128)} fusion(bf16[1024,2048]{0,1:T(8,128)(2,1)} %bitcast.205, bf16[1024,2048]{0,1:T(8,128)(2,1)} %bitcast.206), kind=kOutput, calls=%fused_computation.231 | convolution fusion | flops 8589934592 | bytes 25165824 | tf_op jit(solution)/shard_map/dot_general | solution.py:36
  78.1 3.1 gather_fusion.1
  81.5 124.0 %reduce-scatter.2.cloned.1.call-done = f32[512,2048]{1,0:T(8,128)} async-done(((f32[2048,2048]{1,0:T(8,128)}), f32[512,2048]{1,0:T(8,128)}) %reduce-scatter.2.cloned.1.call-update) | async-done | bytes 4194320 | tf_op jit(solution)/shard_map/reduce_scatter | solution.py:65
  205.4 2.8 select_add_fusion
  209.6 32.1 %all-reduce.21.cloned.1.call-done = (f32[1,128,128]{2,1,0:T(8,128)}, f32[1,128,128]{2,1,0:T(8,128)}, f32[1,128,128]{2,1,0:T(8,128)}) async-done(((f32[1,128,128]{2,1,0:T(8,128)}, f32[1,128,128]{2,1,0:T(8,128)}, f32[1,128,128]{2,1,0:T(8,128)}), (f32[1,128,128]{2,1,0:T(8,128)}, f32[1,128,128]{2,1,0:T(8,128)}, f32[1,128,128]{2,1,0:T(8,128)})) %all-reduce.21.cloned.1.call-update) | async-done | bytes 196624 | tf_op jit(solution)/shard_map/psum | solution.py:87
  242.6 1.5 collective-permute-start
  244.2 3.3 collective-permute-start.1
  247.4 4.8 fusion.123
  252.4 2.1 collective-permute-start.2
  254.5 3.4 collective-permute-start.3
  257.9 4.6 collective-permute-done.2
  262.5 2.5 collective-permute-start.4
  265.5 3.0 collective-permute-start.5
  268.6 3.3 collective-permute-done.4
  271.9 3.1 collective-permute-start.6
  275.1 0.9 collective-permute-done.5
  276.0 6.1 %collective-permute-done.6 = f32[1,3,128,128]{3,2,0,1:T(8,128)S(1)} collective-permute-done((f32[1,3,128,128]{3,2,0,1:T(8,128)S(1)}, f32[1,3,128,128]{3,2,0,1:T(8,128)S(1)}, u32[]{:S(2)}, u32[]{:S(2)}) %collective-permute-start.6) | collective-permute-done | bytes 196640 | tf_op jit(solution)/shard_map/ppermute | solution.py:98
  282.2 1.2 fusion.105
  285.0 1.2 copy.154
  286.2 1.0 copy.156
  287.2 1.0 slice_add_fusion
  289.1 1.0 fusion.24
  290.9 1.0 fusion.23
  292.7 47.7 %custom-call.41 = f32[4,128,128]{2,1,0:T(8,128)S(1)} custom-call(f32[4,128,128]{2,1,0:T(8,128)} %copy.159), custom_call_target="Cholesky" | custom-call | tf_op jit(solution)/shard_map/vmap(jit(cholesky))/cholesky | solution.py:17
  340.7 39.3 %custom-call.42 = f32[4,1,128,128]{2,3,1,0:T(8,128)S(1)} custom-call(f32[4,1,128,128]{3,2,1,0:T(8,128)S(1)} %select_bitcast_fusion.1), custom_call_target="InvertDiagBlocksLowerTriangular" | custom-call | tf_op jit(solution)/shard_map/vmap(jit(_cho_solve))/triangular_solve | solution.py:19
  380.1 1.6 fusion.6
  384.6 1.7 slice_subtract_fusion
  390.8 1.0 fusion.52
  392.5 1.6 fusion.51
  394.1 24.3 %custom-call.43 = f32[2,128,128]{2,1,0:T(8,128)S(1)} custom-call(f32[2,128,128]{2,1,0:T(8,128)} %fusion.51), custom_call_target="Cholesky" | custom-call | tf_op jit(solution)/shard_map/vmap(jit(cholesky))/cholesky | solution.py:17
  419.2 1.5 select_bitcast_fusion.3
  420.7 20.7 %custom-call.44 = f32[2,1,128,128]{2,3,1,0:T(8,128)S(1)} custom-call(f32[2,1,128,128]{3,2,1,0:T(8,128)} %select_bitcast_fusion.3), custom_call_target="InvertDiagBlocksLowerTriangular" | custom-call | tf_op jit(solution)/shard_map/vmap(jit(_cho_solve))/triangular_solve | solution.py:19
  442.0 1.4 fusion.16
  443.4 1.3 fusion.48
  445.0 1.0 convolution_subtract_fusion.1
  446.8 1.7 copy.221
  448.4 1.2 convolution_subtract_fusion.2
  450.3 1.5 fusion.111
  452.0 11.7 %custom-call.49 = f32[1,128,128]{2,1,0:T(8,128)S(1)} custom-call(f32[1,128,128]{2,1,0:T(8,128)S(1)} %fusion.73), custom_call_target="Cholesky" | custom-call | tf_op jit(solution)/shard_map/vmap(jit(cholesky))/cholesky | solution.py:17
  465.0 9.8 %custom-call.50 = f32[1,1,128,128]{2,3,1,0:T(8,128)S(1)} custom-call(f32[1,1,128,128]{3,2,1,0:T(8,128)S(1)} %fusion.55), custom_call_target="InvertDiagBlocksLowerTriangular" | custom-call | tf_op jit(solution)/shard_map/vmap(jit(_cho_solve))/triangular_solve | solution.py:19
  475.5 1.1 fusion.42
  476.6 1.1 convolution_bitcast_fusion.1
  477.8 1.2 fusion.2
  478.9 1.2 fusion.4
  484.9 1.5 fusion.107
  488.7 12.7 %custom-call.51 = f32[1,128,128]{2,1,0:T(8,128)S(1)} custom-call(f32[1,128,128]{2,1,0:T(8,128)} %fusion.66), custom_call_target="Cholesky" | custom-call | tf_op jit(solution)/shard_map/vmap(jit(cholesky))/cholesky | solution.py:17
  502.8 9.8 %custom-call.52 = f32[1,1,128,128]{2,3,1,0:T(8,128)S(1)} custom-call(f32[1,1,128,128]{3,2,1,0:T(8,128)S(1)} %fusion.56), custom_call_target="InvertDiagBlocksLowerTriangular" | custom-call | tf_op jit(solution)/shard_map/vmap(jit(_cho_solve))/triangular_solve | solution.py:19
  513.3 1.2 fusion.45
  514.4 1.1 convolution_bitcast_fusion
  522.0 1.2 copy.186
  523.6 35.2 %custom-call.45 = f32[3,128,128]{2,1,0:T(8,128)S(1)} custom-call(f32[3,128,128]{2,1,0:T(8,128)S(1)} %fusion.34), custom_call_target="Cholesky" | custom-call | tf_op jit(solution)/shard_map/vmap(jit(cholesky))/cholesky | solution.py:17
  560.4 29.5 %custom-call.46 = f32[3,1,128,128]{2,3,1,0:T(8,128)S(1)} custom-call(f32[3,1,128,128]{3,2,1,0:T(8,128)S(1)} %select_bitcast_fusion.2), custom_call_target="InvertDiagBlocksLowerTriangular" | custom-call | tf_op jit(solution)/shard_map/vmap(jit(_cho_solve))/triangular_solve | solution.py:19
  589.9 1.5 fusion.10
  591.9 1.4 slice_subtract_fusion.2
  599.2 2.1 pad.77
  (184 shorter events, 49.5 us)
Async XLA Ops:
  7.2 70.9 %copy-start = (f32[1,2048]{1,0:T(1,128)S(1)}, f32[1,2048]{1,0:T(1,128)}, u32[]{:S(2)}) copy-start(f32[1,2048]{1,0:T(1,128)} %param.16) | copy-start | bytes 24580
  7.2 198.2 %reduce-scatter.2.cloned.1.call-start = ((), (), s32[]{:S(2)}) async-start(), calls=%async_computation.1 | async-start | bytes 20971520 | tf_op jit(solution)/shard_map/reduce_scatter | solution.py:65
  13.6 6.4 %copy-start.21 = (s32[1,8,16]{2,1,0:T(8,128)S(1)}, s32[1,8,16]{2,1,0:T(8,128)}, u32[]{:S(2)}) copy-start(s32[1,8,16]{2,1,0:T(8,128)} %param.13) | copy-start | bytes 1540
  13.6 6.6 %copy-start.23 = (s32[1,16]{1,0:T(1,128)S(1)}, s32[1,16]{1,0:T(1,128)}, u32[]{:S(2)}) copy-start(s32[1,16]{1,0:T(1,128)} %param.14) | copy-start | bytes 196
  13.6 6.8 %copy-start.22 = (s32[16]{0:T(128)S(1)}, s32[16]{0:T(128)}, u32[]{:S(2)}) copy-start(s32[16]{0:T(128)} %param.15) | copy-start | bytes 196
  43.8 5.2 copy-start.20
  76.4 165.3 %all-reduce.21.cloned.1.call-start = ((), (), s32[]{:S(2)}) async-start(), calls=%async_computation.2 | async-start | bytes 393216 | tf_op jit(solution)/shard_map/psum | solution.py:87
  81.3 259.1 %copy-start.16 = (pred[128,128]{1,0:T(8,128)(4,1)}, pred[128,128]{1,0:T(8,128)(4,1)S(1)}, u32[]{:S(2)}) copy-start(pred[128,128]{1,0:T(8,128)(4,1)S(1)} %iota_compare_fusion.3) | copy-start | bytes 49156
  209.6 131.0 %copy-start.15 = (pred[128,128]{1,0:T(8,128)(4,1)}, pred[128,128]{1,0:T(8,128)(4,1)S(1)}, u32[]{:S(2)}) copy-start(pred[128,128]{1,0:T(8,128)(4,1)S(1)} %iota_compare_fusion.4) | copy-start | bytes 49156
  242.6 9.7 %copy-start.17 = (f32[1,128,128]{2,1,0:T(8,128)S(1)}, f32[1,128,128]{2,1,0:T(8,128)}, u32[]{:S(2)}) copy-start(f32[1,128,128]{2,1,0:T(8,128)} %get-tuple-element.15) | copy-start | bytes 196612
  242.6 9.7 %copy-start.18 = (f32[1,128,128]{2,1,0:T(8,128)S(1)}, f32[1,128,128]{2,1,0:T(8,128)}, u32[]{:S(2)}) copy-start(f32[1,128,128]{2,1,0:T(8,128)} %get-tuple-element.16) | copy-start | bytes 196612
  242.6 9.7 %copy-start.19 = (f32[1,128,128]{2,1,0:T(8,128)S(1)}, f32[1,128,128]{2,1,0:T(8,128)}, u32[]{:S(2)}) copy-start(f32[1,128,128]{2,1,0:T(8,128)} %get-tuple-element.17) | copy-start | bytes 196612
  242.6 9.8 %collective-permute-start = (f32[1,3,128,128]{3,2,0,1:T(8,128)S(1)}, f32[1,3,128,128]{3,2,0,1:T(8,128)S(1)}, u32[]{:S(2)}, u32[]{:S(2)}) collective-permute-start(f32[1,3,128,128]{3,2,0,1:T(8,128)S(1)} %maximum_bitcast_fusion), channel_id=1, source_target_pairs={{0,4},{4,8},{8,12},{12,16},{16,20},{20,24},{24,28},{28,0},{1,5},{5... | collective-permute-start | bytes 589832 | tf_op jit(solution)/shard_map/ppermute | solution.py:98
  244.2 10.3 %collective-permute-start.1 = (f32[1,3,128,128]{3,2,0,1:T(8,128)S(1)}, f32[1,3,128,128]{3,2,0,1:T(8,128)S(1)}, u32[]{:S(2)}, u32[]{:S(2)}) collective-permute-start(f32[1,3,128,128]{3,2,0,1:T(8,128)S(1)} %maximum_bitcast_fusion), channel_id=1, source_target_pairs={{0,28},{4,0},{8,4},{12,8},{16,12},{20,16},{24,20},{28,24},{1,29},{... | collective-permute-start | bytes 589832 | tf_op jit(solution)/shard_map/ppermute | solution.py:103
  252.4 10.1 %collective-permute-start.2 = (f32[1,3,128,128]{3,2,0,1:T(8,128)S(1)}, f32[1,3,128,128]{3,2,0,1:T(8,128)S(1)}, u32[]{:S(2)}, u32[]{:S(2)}) collective-permute-start(f32[1,3,128,128]{3,2,0,1:T(8,128)S(1)} %collective-permute-done), channel_id=1, source_target_pairs={{0,4},{4,8},{8,12},{12,16},{16,20},{20,24},{24,28},{28,0},{1,5},{5... | collective-permute-start | bytes 589832 | tf_op jit(solution)/shard_map/ppermute | solution.py:98
  254.5 11.0 %collective-permute-start.3 = (f32[1,3,128,128]{3,2,0,1:T(8,128)S(1)}, f32[1,3,128,128]{3,2,0,1:T(8,128)S(1)}, u32[]{:S(2)}, u32[]{:S(2)}) collective-permute-start(f32[1,3,128,128]{3,2,0,1:T(8,128)S(1)} %collective-permute-done.1), channel_id=1, source_target_pairs={{0,28},{4,0},{8,4},{12,8},{16,12},{20,16},{24,20},{28,24},{1,29},{... | collective-permute-start | bytes 589832 | tf_op jit(solution)/shard_map/ppermute | solution.py:103
  262.5 9.4 %collective-permute-start.4 = (f32[1,3,128,128]{3,2,0,1:T(8,128)S(1)}, f32[1,3,128,128]{3,2,0,1:T(8,128)S(1)}, u32[]{:S(2)}, u32[]{:S(2)}) collective-permute-start(f32[1,3,128,128]{3,2,0,1:T(8,128)S(1)} %collective-permute-done.2), channel_id=1, source_target_pairs={{0,4},{4,8},{8,12},{12,16},{16,20},{20,24},{24,28},{28,0},{1,5},{5... | collective-permute-start | bytes 589832 | tf_op jit(solution)/shard_map/ppermute | solution.py:98
  265.5 10.5 %collective-permute-start.5 = (f32[1,3,128,128]{3,2,0,1:T(8,128)S(1)}, f32[1,3,128,128]{3,2,0,1:T(8,128)S(1)}, u32[]{:S(2)}, u32[]{:S(2)}) collective-permute-start(f32[1,3,128,128]{3,2,0,1:T(8,128)S(1)} %collective-permute-done.3), channel_id=1, source_target_pairs={{0,28},{4,0},{8,4},{12,8},{16,12},{20,16},{24,20},{28,24},{1,29},{... | collective-permute-start | bytes 589832 | tf_op jit(solution)/shard_map/ppermute | solution.py:103
  271.9 10.3 %collective-permute-start.6 = (f32[1,3,128,128]{3,2,0,1:T(8,128)S(1)}, f32[1,3,128,128]{3,2,0,1:T(8,128)S(1)}, u32[]{:S(2)}, u32[]{:S(2)}) collective-permute-start(f32[1,3,128,128]{3,2,0,1:T(8,128)S(1)} %collective-permute-done.4), channel_id=1, source_target_pairs={{0,4},{4,8},{8,12},{12,16},{16,20},{20,24},{24,28},{28,0},{1,5},{5... | collective-permute-start | bytes 589832 | tf_op jit(solution)/shard_map/ppermute | solution.py:98
  287.2 92.8 %copy-start.5 = (f32[4,128,128]{1,2,0:T(8,128)S(1)}, f32[4,128,128]{1,2,0:T(8,128)}, u32[]{:S(2)}) copy-start(f32[4,128,128]{1,2,0:T(8,128)} %copy.220) | copy-start | bytes 786436
  384.6 56.8 %copy-start.1 = (f32[4,128,128]{1,2,0:T(8,128)}, f32[4,128,128]{1,2,0:T(8,128)S(1)}, u32[]{:S(2)}) copy-start(f32[4,128,128]{1,2,0:T(8,128)S(1)} %slice_subtract_fusion.1) | copy-start | bytes 786436
  389.4 0.7 copy-start.4
  441.4 0.7 copy-start.12
  445.0 1.7 copy-start.2
  449.6 0.7 copy-start.6
  474.8 0.6 copy-start.13
  477.7 39.9 %copy-start.8 = (f32[1,128,256]{2,1,0:T(8,128)}, f32[1,128,256]{2,1,0:T(8,128)S(1)}, u32[]{:S(2)}) copy-start(f32[1,128,256]{2,1,0:T(8,128)S(1)} %convolution_bitcast_fusion.1) | copy-start | bytes 393220
  512.6 0.6 copy-start.14
  515.6 2.1 copy-start.10
  522.0 71.9 %copy-start.3 = (f32[2,128,128]{2,1,0:T(8,128)S(1)}, f32[2,128,128]{2,1,0:T(8,128)}, u32[]{:S(2)}) copy-start(f32[2,128,128]{2,1,0:T(8,128)} %copy-done.2) | copy-start | bytes 393220
  522.0 71.9 %copy-start.7 = (f32[2,128,128]{2,1,0:T(8,128)S(1)}, f32[2,128,128]{2,1,0:T(8,128)}, u32[]{:S(2)}) copy-start(f32[2,128,128]{2,1,0:T(8,128)} %copy-done.6) | copy-start | bytes 393220
  522.0 71.9 %copy-start.9 = (f32[1,128,256]{2,1,0:T(8,128)S(1)}, f32[1,128,256]{2,1,0:T(8,128)}, u32[]{:S(2)}) copy-start(f32[1,128,256]{2,1,0:T(8,128)} %copy-done.8) | copy-start | bytes 393220
  522.0 73.1 %copy-start.11 = (f32[1,128,256]{2,1,0:T(8,128)S(1)}, f32[1,128,256]{2,1,0:T(8,128)}, u32[]{:S(2)}) copy-start(f32[1,128,256]{2,1,0:T(8,128)} %copy-done.10) | copy-start | bytes 393220
Sparse Core Ops, SparseCore 0:
  76.6 128.8 reduce-scatter.1
  209.7 31.9 all-reduce.20
